TPU v7x, 256 devices: a whole 4x4x8 slice. The times are simulated.
256 devices in a mesh: dp: 8 (over y, core), expert: 32 (over z, x).
Axes of the slice: x: 4, y: 4, z: 8, core: 2. Of those that a mesh axis runs over, the one named last changes fastest.
Arguments:
- tokens: bfloat16 [4096, 4096], P('expert', 'dp'), may hold values from -6 to 6
- expert_ids: int32 [4096, 8], P('expert'), may hold values from 0 to 63, all different within a row; in each aligned block of 128 rows (0 to 127, 128 to 255, ...) at most 24 rows name the same one
- route_weights: float32 [4096, 8], P('expert'), may hold values from 0.1 to 0.4
- gate_up_weight: bfloat16 [64, 4096, 1536], P('expert', 'dp'), may hold values from -0.09375 to 0.09375
- down_weight: bfloat16 [64, 768, 4096], P('expert', None, 'dp'), may hold values from -0.21875 to 0.21875
- out_grad: bfloat16 [4096, 4096], P('expert', 'dp'), may hold values from -6 to 6
Outputs:
- layer_out: bfloat16 [4096, 4096], P('expert', 'dp')
- token_grad: bfloat16 [4096, 4096], P('expert', 'dp')
- route_grad: float32 [4096, 8], P('expert')
- gate_up_grad: bfloat16 [64, 4096, 1536], P('expert', 'dp')
- down_grad: bfloat16 [64, 768, 4096], P('expert', None, 'dp')
Inputs may be any that keep to these rules, and one draw needn't show every extreme that they name: `expert_ids`: each row names 8 different experts. Among the 128 rows of one group no expert is named more than 24 times, and in every draw some group names some expert exactly 24 times.
All inputs are finite; a program needn't handle non-finite values.
Results may differ from a plain program's by a relative error of at most 0.029.
Values may be sent and summed in bfloat16 or wider, within the bound.
No kernel may reach another device: no remote copies, remote signals or barrier semaphores. Data moves between devices by JAX's collectives and lax.ppermute only.
A program may use at most 128 MiB of HBM per device.

v0:
```python
import jax
import jax.numpy as jnp
from jax import lax
from jax.sharding import PartitionSpec as P


def local(tokens, expert_ids, route_weights, gate_up_weight, down_weight, out_grad):
    tok_count, piece_width = tokens.shape
    top_count = expert_ids.shape[1]
    group_count = lax.axis_size("expert")
    local_count = gate_up_weight.shape[0]
    hidden_units = down_weight.shape[1]
    expert_total = local_count * group_count
    capacity = 3 * tok_count * top_count // (2 * expert_total)
    slot_count = expert_total * capacity
    rows_all = group_count * capacity
    route_count = tok_count * top_count
    block_shape = (local_count, group_count, capacity, piece_width)
    route_ids = expert_ids.reshape(-1)
    onehot = (route_ids[:, None] == jnp.arange(expert_total, dtype=jnp.int32)[None, :]).astype(
        jnp.bfloat16
    )
    order = jnp.arange(route_count, dtype=jnp.int32)
    lower = (order[None, :] < order[:, None]).astype(jnp.bfloat16)
    earlier = jnp.dot(lower, onehot, preferred_element_type=jnp.float32)
    slot_rank = jnp.sum(onehot.astype(jnp.float32) * earlier, axis=1).astype(jnp.int32)
    slot_index = (
        route_ids % local_count * rows_all + route_ids // local_count * capacity + slot_rank
    )
    route_hit = slot_index[:, None] == jnp.arange(slot_count, dtype=jnp.int32)[None, :]
    token_hit = jnp.any(route_hit.reshape(tok_count, top_count, slot_count), axis=1).astype(
        jnp.bfloat16
    )
    weight_flat = route_weights.reshape(-1)
    slot_weight = jnp.sum(jnp.where(route_hit, weight_flat[:, None], 0.0), axis=0)
    outbound = lax.dot_general(
        token_hit, tokens, (((0,), (0,)), ((), ())), preferred_element_type=jnp.float32
    ).astype(jnp.bfloat16)
    grad_outbound = (
        slot_weight[:, None]
        * lax.dot_general(
            token_hit, out_grad, (((0,), (0,)), ((), ())), preferred_element_type=jnp.float32
        )
    ).astype(jnp.bfloat16)
    both = jnp.stack([outbound, grad_outbound]).reshape((2,) + block_shape)
    both = lax.all_to_all(both, "expert", split_axis=2, concat_axis=2, tiled=True)
    arrived = both[0].reshape(local_count, rows_all, piece_width)
    grad_arrived = both[1].reshape(local_count, rows_all, piece_width)
    gate_up_part = jnp.einsum(
        "lrk,lkf->rlf", arrived, gate_up_weight, preferred_element_type=jnp.float32
    ).astype(jnp.bfloat16)
    hidden_grad_part = jnp.einsum(
        "lrk,lfk->rlf", grad_arrived, down_weight, preferred_element_type=jnp.float32
    ).astype(jnp.bfloat16)
    summed = lax.psum_scatter(
        jnp.concatenate([gate_up_part, hidden_grad_part], axis=2),
        "dp",
        scatter_dimension=0,
        tiled=True,
    ).astype(jnp.float32)
    gate_pre = summed[..., :hidden_units]
    up_pre = summed[..., hidden_units : 2 * hidden_units]
    hidden_grad = summed[..., 2 * hidden_units :]
    sigmoid_gate = jax.nn.sigmoid(gate_pre)
    activation = gate_pre * sigmoid_gate
    hidden_mine = (activation * up_pre).astype(jnp.bfloat16)
    gate_grad = hidden_grad * up_pre * sigmoid_gate * (1.0 + gate_pre * (1.0 - sigmoid_gate))
    up_grad = hidden_grad * activation
    preact_grad = jnp.concatenate([gate_grad, up_grad], axis=2).astype(jnp.bfloat16)
    hidden_all = lax.all_gather(hidden_mine, "dp", axis=0, tiled=True)
    preact_grad_all = lax.all_gather(preact_grad, "dp", axis=0, tiled=True)
    out_slice = jnp.einsum(
        "rlf,lfk->lrk", hidden_all, down_weight, preferred_element_type=jnp.float32
    ).astype(jnp.bfloat16)
    grad_routes = jnp.repeat(out_grad, top_count, axis=0).astype(jnp.float32)
    returned = lax.all_to_all(
        out_slice.reshape(block_shape), "expert", split_axis=1, concat_axis=1, tiled=True
    )
    route_pick = route_hit.astype(jnp.bfloat16)
    y_routes = jnp.dot(
        route_pick, returned.reshape(slot_count, piece_width), preferred_element_type=jnp.float32
    )
    layer_out = (
        (weight_flat[:, None] * y_routes)
        .reshape(tok_count, top_count, piece_width)
        .sum(axis=1)
        .astype(jnp.bfloat16)
    )
    partial_dot = jnp.sum(grad_routes * y_routes, axis=1).reshape(tok_count, top_count)
    route_grad = lax.psum(partial_dot, "dp")
    x_grad_slice = jnp.einsum(
        "rlf,lkf->lrk", preact_grad_all, gate_up_weight, preferred_element_type=jnp.float32
    ).astype(jnp.bfloat16)
    gate_up_grad = jnp.einsum(
        "lrk,rlf->lkf", arrived, preact_grad_all, preferred_element_type=jnp.float32
    ).astype(jnp.bfloat16)
    down_grad = jnp.einsum(
        "rlf,lrk->lfk", hidden_all, grad_arrived, preferred_element_type=jnp.float32
    ).astype(jnp.bfloat16)
    grad_back = lax.all_to_all(
        x_grad_slice.reshape(block_shape), "expert", split_axis=1, concat_axis=1, tiled=True
    )
    token_grad = jnp.dot(
        token_hit, grad_back.reshape(slot_count, piece_width), preferred_element_type=jnp.float32
    ).astype(jnp.bfloat16)
    return (layer_out, token_grad, route_grad, gate_up_grad, down_grad)


def solution(mesh):
    placed = (
        P("expert", "dp"),
        P("expert", None),
        P("expert", None),
        P("expert", "dp", None),
        P("expert", None, "dp"),
        P("expert", "dp"),
    )
    return jax.shard_map(
        local,
        mesh=mesh,
        in_specs=placed,
        out_specs=(
            P("expert", "dp"),
            P("expert", "dp"),
            P("expert", None),
            P("expert", "dp", None),
            P("expert", None, "dp"),
        ),
        check_vma=False,
    )
```

profile of v0, /device:TPU:4, one launch (start us, length us, event | category | flops | bytes accessed | tf_op | source)
XLA Modules:
  0.0 303.9 jit_solution(3204589052721626172)
XLA Ops:
  9.9 3.2 %fusion.1 = pred[128,1536]{1,0:T(8,128)(4,1)S(1)} fusion(s32[128,8]{1,0:T(8,128)S(1)} %fusion.13), kind=kLoop, calls=%fused_computation.5 | loop fusion | flops 2949120 | bytes 200704 | tf_op jit(solution)/shard_map/reduce_or | solution.py:31
  13.9 1.5 convolution_convert_fusion.1
  16.9 84.4 %all_to_all.15 = bf16[2,2,32,24,512]{4,3,1,0,2:T(8,128)(2,1)S(1)} all-to-all(bf16[2,2,32,24,512]{4,3,1,0,2:T(8,128)(2,1)S(1)} %copy.74), channel_id=1, replica_groups=mesh['dp'=8,'expert'=32] {'expert'}, dimensions={2} | all-to-all | bytes 6291456 | tf_op jit(solution)/shard_map/all_to_all | solution.py:46
  101.8 4.2 %convert_bitcast_fusion = bf16[768,2,1536]{2,0,1:T(8,128)(2,1)} fusion(bf16[2,768,512]{2,1,0:T(8,128)(2,1)S(1)} %bitcast.40, bf16[2,512,1536]{2,1,0:T(8,128)(2,1)S(1)} %copy-done), kind=kOutput, calls=%fused_computation.6 | convolution fusion | flops 2418278400 | bytes 9437184 | tf_op jit(solution)/shard_map/lrk,lkf->rlf/dot_general | solution.py:49
  106.0 2.8 convert_bitcast_fusion.1
  108.9 6.4 %pad_maximum_fusion = bf16[768,2,2304]{2,0,1:T(8,128)(2,1)} fusion(bf16[768,2,768]{2,0,1:T(8,128)(2,1)} %convert_bitcast_fusion.1, bf16[768,2,1536]{2,0,1:T(8,128)(2,1)} %convert_bitcast_fusion), kind=kLoop, calls=%fused_computation | loop fusion | flops 14155776 | bytes 14155776 | tf_op jit(solution)/shard_map/concatenate | solution.py:56
  115.4 45.8 %reduce-scatter.2.cloned.1.call-done = bf16[96,2,2304]{2,0,1:T(8,128)(2,1)} async-done(((bf16[768,2,2304]{2,0,1:T(8,128)(2,1)}), bf16[96,2,2304]{2,0,1:T(8,128)(2,1)}) %reduce-scatter.2.cloned.1.call-update) | async-done | bytes 884752 | tf_op jit(solution)/shard_map/reduce_scatter | solution.py:55
  161.2 1.3 convert_element_type.80
  163.7 1.9 pad_maximum_fusion.2
  165.6 26.0 %all-gather.3.cloned.1.call-done = bf16[768,2,768]{2,0,1:T(8,128)(2,1)} async-done(((bf16[96,2,768]{2,0,1:T(8,128)(2,1)}), bf16[768,2,768]{2,0,1:T(8,128)(2,1)}) %all-gather.3.cloned.1.call-update) | async-done | bytes 2359312 | tf_op jit(solution)/shard_map/all_gather | solution.py:70
  191.6 3.5 %convolution_convert_fusion.3 = bf16[2,768,512]{2,1,0:T(8,128)(2,1)S(1)} fusion(bf16[768,2,768]{2,0,1:T(8,128)(2,1)} %all-gather.3.cloned.1.call-done, bf16[2,768,512]{2,1,0:T(8,128)(2,1)} %param.10), kind=kOutput, calls=%fused_computation.20 | convolution fusion | flops 1208745984 | bytes 5505024 | tf_op jit(solution)/shard_map/rlf,lfk->lrk/dot_general | solution.py:72
  195.1 1.4 copy.66
  196.5 10.2 %all-to-all-start.1 = ((bf16[2,32,24,512]{3,2,0,1:T(8,128)(2,1)}), bf16[2,32,24,512]{3,2,0,1:T(8,128)(2,1)}, u32[]{:S(2)}, u32[]{:S(2)}) async-start(bf16[2,32,24,512]{3,2,0,1:T(8,128)(2,1)} %copy.66), calls=%async_computation.2 | async-start | bytes 3145728 | tf_op jit(solution)/shard_map/all_to_all | solution.py:76
  206.7 24.8 %all-gather.5.cloned.1.call-done = bf16[768,2,1536]{2,0,1:T(8,128)(2,1)} async-done(((bf16[96,2,1536]{2,0,1:T(8,128)(2,1)}), bf16[768,2,1536]{2,0,1:T(8,128)(2,1)}) %all-gather.5.cloned.1.call-update) | async-done | bytes 4718608 | tf_op jit(solution)/shard_map/all_gather | solution.py:71
  231.4 5.0 %convolution_convert_fusion.4 = bf16[2,768,512]{2,1,0:T(8,128)(2,1)S(1)} fusion(bf16[768,2,1536]{2,0,1:T(8,128)(2,1)} %all-gather.5.cloned.1.call-done, bf16[2,512,1536]{2,1,0:T(8,128)(2,1)S(1)} %copy-done), kind=kOutput, calls=%fused_computation.21 | convolution fusion | flops 2416705536 | bytes 9437184 | tf_op jit(solution)/shard_map/rlf,lkf->lrk/dot_general | solution.py:91
  236.4 1.4 copy.68
  237.8 8.6 %all-to-all-done.1 = bf16[2,32,24,512]{3,2,0,1:T(8,128)(2,1)} async-done(((bf16[2,32,24,512]{3,2,0,1:T(8,128)(2,1)}), bf16[2,32,24,512]{3,2,0,1:T(8,128)(2,1)}, u32[]{:S(2)}, u32[]{:S(2)}) %all-to-all-start.1) | async-done | bytes 1572896 | tf_op jit(solution)/shard_map/all_to_all | solution.py:76
  246.4 5.6 %all-to-all-start.2 = ((bf16[2,32,24,512]{3,2,0,1:T(8,128)(2,1)}), bf16[2,32,24,512]{3,2,0,1:T(8,128)(2,1)}, u32[]{:S(2)}, u32[]{:S(2)}) async-start(bf16[2,32,24,512]{3,2,0,1:T(8,128)(2,1)} %copy.68), calls=%async_computation.3 | async-start | bytes 3145728 | tf_op jit(solution)/shard_map/all_to_all | solution.py:100
  252.0 4.7 %convolution_convert_fusion.2 = bf16[2,768,512]{2,1,0:T(8,128)(2,1)} fusion(bf16[768,2,768]{2,0,1:T(8,128)(2,1)} %all-gather.3.cloned.1.call-done, bf16[2,768,512]{2,1,0:T(8,128)(2,1)} %bitcast.43), kind=kOutput, calls=%fused_computation.19 | convolution fusion | flops 1208745984 | bytes 5505024 | tf_op jit(solution)/shard_map/rlf,lrk->lfk/dot_general | solution.py:97
  256.7 1.5 copy.67
  258.3 2.9 bitcast_reduce_fusion
  261.5 25.5 %psum.7 = f32[128,8]{1,0:T(8,128)S(1)} all-reduce(f32[128,8]{1,0:T(8,128)S(1)} %reshape.113), channel_id=1, replica_groups=mesh['dp'=8,'expert'=32] {'dp'}, use_global_device_ids=true, to_apply=%region_6.7 | all-reduce | flops 1024 | bytes 8192 | tf_op jit(solution)/shard_map/psum | solution.py:90
  287.7 7.1 %convolution_convert_fusion = bf16[2,512,1536]{2,1,0:T(8,128)(2,1)} fusion(bf16[2,768,512]{2,1,0:T(8,128)(2,1)} %bitcast.41, bf16[768,2,1536]{2,0,1:T(8,128)(2,1)} %all-gather.5.cloned.1.call-done), kind=kOutput, calls=%fused_computation.9 | convolution fusion | flops 2417491968 | bytes 9437184 | tf_op jit(solution)/shard_map/lrk,rlf->lkf/dot_general | solution.py:94
  294.8 1.5 copy.69
  (39 shorter events, 8.8 us)
Async XLA Ops:
  7.2 94.6 %copy-start = (bf16[2,512,1536]{2,1,0:T(8,128)(2,1)S(1)}, bf16[2,512,1536]{2,1,0:T(8,128)(2,1)}, u32[]{:S(2)}) copy-start(bf16[2,512,1536]{2,1,0:T(8,128)(2,1)} %param.9) | copy-start | bytes 9437188
  7.2 154.0 %reduce-scatter.2.cloned.1.call-start = ((), (), s32[]{:S(2)}) async-start(), calls=%async_computation.4 | async-start | bytes 7962624 | tf_op jit(solution)/shard_map/reduce_scatter | solution.py:55
  8.3 7.2 %copy-start.3 = (bf16[128,512]{1,0:T(8,128)(2,1)S(1)}, bf16[128,512]{1,0:T(8,128)(2,1)}, u32[]{:S(2)}) copy-start(bf16[128,512]{1,0:T(8,128)(2,1)} %param.11) | copy-start | bytes 393220
  101.7 4.4 %copy-start.1 = (bf16[1,2,32,24,512]{4,3,2,1,0:T(8,128)(2,1)}, bf16[1,2,32,24,512]{4,3,2,1,0:T(8,128)(2,1)S(1)}, u32[]{:S(2)}) copy-start(bf16[1,2,32,24,512]{4,3,2,1,0:T(8,128)(2,1)S(1)} %copy.63) | copy-start | bytes 4718596
  101.8 4.2 %copy-start.2 = (bf16[1,2,32,24,512]{4,3,2,1,0:T(8,128)(2,1)}, bf16[1,2,32,24,512]{4,3,2,1,0:T(8,128)(2,1)S(1)}, u32[]{:S(2)}) copy-start(bf16[1,2,32,24,512]{4,3,2,1,0:T(8,128)(2,1)S(1)} %copy.64) | copy-start | bytes 4718596
  101.8 4.2 %copy-start.4 = (bf16[2,768,512]{2,1,0:T(8,128)(2,1)S(1)}, bf16[2,768,512]{2,1,0:T(8,128)(2,1)}, u32[]{:S(2)}) copy-start(bf16[2,768,512]{2,1,0:T(8,128)(2,1)} %param.10) | copy-start | bytes 4718596
  115.3 76.3 %all-gather.3.cloned.1.call-start = ((), (), s32[]{:S(2)}) async-start(), calls=%async_computation.5 | async-start | bytes 2654208 | tf_op jit(solution)/shard_map/all_gather | solution.py:70
  163.7 67.8 %all-gather.5.cloned.1.call-start = ((), (), s32[]{:S(2)}) async-start(), calls=%async_computation.6 | async-start | bytes 5308416 | tf_op jit(solution)/shard_map/all_gather | solution.py:71
  196.5 49.9 %all-to-all-start.1 = ((bf16[2,32,24,512]{3,2,0,1:T(8,128)(2,1)}), bf16[2,32,24,512]{3,2,0,1:T(8,128)(2,1)}, u32[]{:S(2)}, u32[]{:S(2)}) async-start(bf16[2,32,24,512]{3,2,0,1:T(8,128)(2,1)} %copy.66), calls=%async_computation.2 | async-start | bytes 3145728 | tf_op jit(solution)/shard_map/all_to_all | solution.py:76
  246.4 48.4 %all-to-all-start.2 = ((bf16[2,32,24,512]{3,2,0,1:T(8,128)(2,1)}), bf16[2,32,24,512]{3,2,0,1:T(8,128)(2,1)}, u32[]{:S(2)}, u32[]{:S(2)}) async-start(bf16[2,32,24,512]{3,2,0,1:T(8,128)(2,1)} %copy.68), calls=%async_computation.3 | async-start | bytes 3145728 | tf_op jit(solution)/shard_map/all_to_all | solution.py:100
Sparse Core Ops, SparseCore 0:
  115.4 45.7 reduce-scatter.1
  163.8 27.7 all-gather.2
  194.0 37.3 all-gather.4
where the time goes:
time: 304 us
  blocking collectives  110 us (36%)
  waiting for transfers between devices  105 us (35%)
  matrix products  34 us (11%)
  starting transfers between devices  15.9 us (5%)
  other arithmetic  15.4 us (5%)
  between operations  14 us (5%)
  local copies, waits for them, and re-layouts  9.53 us (3%)
    all_to_all x1, blocking collectives, local(): lax.all_to_all(both, 'expert', split_axis=2, concat_axis=2, tiled=True)  84.4 us
    reduce_scatter x1, waiting for transfers between devices, local(): lax.psum_scatter(jnp.concatenate([gate_up_part, hidden_grad_part], axis=2...  45.8 us
    all_gather x1, waiting for transfers between devices, local(): hidden_all = lax.all_gather(hidden_mine, 'dp', axis=0, tiled=True)  26 us
    psum x1, blocking collectives, local(): route_grad = lax.psum(partial_dot, 'dp')  25.5 us
    all_gather x1, waiting for transfers between devices, local(): preact_grad_all = lax.all_gather(preact_grad, 'dp', axis=0, tiled=True)  24.8 us
    all_to_all x1, starting transfers between devices, local(): lax.all_to_all(out_slice.reshape(block_shape), 'expert', split_axis=1, co...  10.2 us
    all_to_all x1, waiting for transfers between devices, local(): lax.all_to_all(out_slice.reshape(block_shape), 'expert', split_axis=1, co...  8.58 us
    dot_general x1, matrix products, local(): jnp.einsum('lrk,rlf->lkf', arrived, preact_grad_all, preferred_element_ty...  7.12 us
  transfers between devices with their start and end apart: 5, of which 4 were waited for; matrix products, arithmetic and copies ran while one was open for 10% of the time, Pallas kernels for 0%

commit v1 on v0

--- a/solution.py
+++ b/solution.py
@@ -68,7 +68,21 @@
     up_grad = hidden_grad * activation
     preact_grad = jnp.concatenate([gate_grad, up_grad], axis=2).astype(jnp.bfloat16)
     hidden_all = lax.all_gather(hidden_mine, "dp", axis=0, tiled=True)
-    preact_grad_all = lax.all_gather(preact_grad, "dp", axis=0, tiled=True)
+    ways, here, step = (lax.axis_size("dp"), lax.axis_index("dp"), preact_grad.shape[0])
+    dims = [n * ways if d == 0 else n for d, n in enumerate(preact_grad.shape)]
+    full = lax.dynamic_update_slice_in_dim(
+        jnp.zeros(dims, preact_grad.dtype), preact_grad, here * step, axis=0
+    )
+    going_up = going_down = preact_grad
+    for far in range(1, ways // 2 + 1):
+        going_up = lax.ppermute(going_up, "dp", [(d, (d + 1) % ways) for d in range(ways)])
+        full = lax.dynamic_update_slice_in_dim(full, going_up, (here - far) % ways * step, axis=0)
+        if 2 * far < ways:
+            going_down = lax.ppermute(going_down, "dp", [(d, (d - 1) % ways) for d in range(ways)])
+            full = lax.dynamic_update_slice_in_dim(
+                full, going_down, (here + far) % ways * step, axis=0
+            )
+    preact_grad_all = full
     out_slice = jnp.einsum(
         "rlf,lfk->lrk", hidden_all, down_weight, preferred_element_type=jnp.float32
     ).astype(jnp.bfloat16)

time: 304 us -> 348 us (1.14)
  waiting for transfers between devices: 105 us -> 124 us
  local copies, waits for them, and re-layouts: 9.53 us -> 19.5 us
  starting transfers between devices: 15.9 us -> 24.8 us
  blocking collectives: 110 us -> 118 us
    ppermute x0 -> x7, waiting for transfers between devices: none -> 31.5 us  [the longest x4 31.3 us: local(): lax.ppermute(going_up, 'dp', [(d, (d + 1) % ways) for d in range(ways)])]
    all_to_all x1, waiting for transfers between devices: 0.01 us -> 26.8 us  [local(): lax.all_to_all(x_grad_slice.reshape(block_shape), 'expert', split_axis=1,...]
    all_gather x1, waiting for transfers between devices: 26 us -> 0.02 us  [local(): hidden_all = lax.all_gather(hidden_mine, 'dp', axis=0, tiled=True)]
    all_gather x1 -> x0, waiting for transfers between devices: 24.8 us -> none  [local(): preact_grad_all = lax.all_gather(preact_grad, 'dp', axis=0, tiled=True)]
    all_to_all x1, waiting for transfers between devices: 8.58 us -> 19.9 us  [local(): lax.all_to_all(out_slice.reshape(block_shape), 'expert', split_axis=1, co...]
    dynamic_update_slice x0 -> x7, local copies, waits for them, and re-layouts: none -> 10.3 us  [the longest x4 5.57 us: local(): lax.dynamic_update_slice_in_dim(full, going_up, (here - far) % ways * ste...]
    ppermute x0 -> x7, starting transfers between devices: none -> 8.87 us  [the longest x3 8.85 us: local(): lax.ppermute(going_down, 'dp', [(d, (d - 1) % ways) for d in range(ways)])]
    psum x1, blocking collectives: 25.5 us -> 33.9 us  [local(): route_grad = lax.psum(partial_dot, 'dp')]
  transfers between devices with their start and end apart: 5 -> 11, of which waited for: 4 -> 8; matrix products, arithmetic and copies ran while one was open for 10% -> 10% of each run, Pallas kernels for 0% -> 0%
where the time goes in v1:
time: 348 us
  waiting for transfers between devices  124 us (36%)
  blocking collectives  118 us (34%)
  matrix products  32 us (9%)
  starting transfers between devices  24.8 us (7%)
  local copies, waits for them, and re-layouts  19.5 us (6%)
  other arithmetic  15 us (4%)
  between operations  14.3 us (4%)
    all_to_all x1, blocking collectives, local(): lax.all_to_all(both, 'expert', split_axis=2, concat_axis=2, tiled=True)  84.4 us
    reduce_scatter x1, waiting for transfers between devices, local(): lax.psum_scatter(jnp.concatenate([gate_up_part, hidden_grad_part], axis=2...  45.6 us
    psum x1, blocking collectives, local(): route_grad = lax.psum(partial_dot, 'dp')  33.9 us
    ppermute x4, waiting for transfers between devices, local(): lax.ppermute(going_up, 'dp', [(d, (d + 1) % ways) for d in range(ways)])  31.3 us
    all_to_all x1, waiting for transfers between devices, local(): lax.all_to_all(x_grad_slice.reshape(block_shape), 'expert', split_axis=1,...  26.8 us
    all_to_all x1, waiting for transfers between devices, local(): lax.all_to_all(out_slice.reshape(block_shape), 'expert', split_axis=1, co...  19.9 us
    all_to_all x1, starting transfers between devices, local(): lax.all_to_all(x_grad_slice.reshape(block_shape), 'expert', split_axis=1,...  10.1 us
    ppermute x3, starting transfers between devices, local(): lax.ppermute(going_down, 'dp', [(d, (d - 1) % ways) for d in range(ways)])  8.85 us
  transfers between devices with their start and end apart: 11, of which 8 were waited for; matrix products, arithmetic and copies ran while one was open for 10% of the time, Pallas kernels for 0%

profile of v1, /device:TPU:4, one launch (start us, length us, event | category | flops | bytes accessed | tf_op | source)
XLA Modules:
  0.0 347.7 jit_solution(15119195057405333035)
XLA Ops:
  10.0 3.2 fusion.1
  16.9 84.4 %all_to_all.15 = bf16[2,2,32,24,512]{4,3,1,0,2:T(8,128)(2,1)S(1)} all-to-all(bf16[2,2,32,24,512]{4,3,1,0,2:T(8,128)(2,1)S(1)} %copy.74), channel_id=1, replica_groups=mesh['dp'=8,'expert'=32] {'expert'}, dimensions={2} | all-to-all | bytes 6291456 | tf_op jit(solution)/shard_map/all_to_all | solution.py:46
  101.8 4.2 %convert_bitcast_fusion = bf16[768,2,1536]{2,0,1:T(8,128)(2,1)} fusion(bf16[2,768,512]{2,1,0:T(8,128)(2,1)S(1)} %bitcast.40, bf16[2,512,1536]{2,1,0:T(8,128)(2,1)S(1)} %copy-done), kind=kOutput, calls=%fused_computation.6 | convolution fusion | flops 2418278400 | bytes 9437184 | tf_op jit(solution)/shard_map/lrk,lkf->rlf/dot_general | solution.py:49
  106.1 2.8 convert_bitcast_fusion.1
  108.9 6.4 %pad_maximum_fusion = bf16[768,2,2304]{2,0,1:T(8,128)(2,1)} fusion(bf16[768,2,768]{2,0,1:T(8,128)(2,1)} %convert_bitcast_fusion.1, bf16[768,2,1536]{2,0,1:T(8,128)(2,1)} %convert_bitcast_fusion), kind=kLoop, calls=%fused_computation | loop fusion | flops 14155776 | bytes 14155776 | tf_op jit(solution)/shard_map/concatenate | solution.py:56
  115.6 45.6 %reduce-scatter.2.cloned.1.call-done = bf16[96,2,2304]{2,0,1:T(8,128)(2,1)} async-done(((bf16[768,2,2304]{2,0,1:T(8,128)(2,1)}), bf16[96,2,2304]{2,0,1:T(8,128)(2,1)}) %reduce-scatter.2.cloned.1.call-update) | async-done | bytes 884752 | tf_op jit(solution)/shard_map/reduce_scatter | solution.py:55
  163.5 2.4 broadcast_in_dim.26
  166.9 3.0 collective-permute-start.1
  169.9 7.7 %collective-permute-done = bf16[96,2,1536]{2,0,1:T(8,128)(2,1)} collective-permute-done((bf16[96,2,1536]{2,0,1:T(8,128)(2,1)S(1)}, bf16[96,2,1536]{2,0,1:T(8,128)(2,1)}, u32[]{:S(2)}, u32[]{:S(2)}) %collective-permute-start) | collective-permute-done | bytes 589856 | tf_op jit(solution)/shard_map/ppermute | solution.py:78
  177.5 3.0 collective-permute-start.3
  180.5 7.8 %collective-permute-done.2 = bf16[96,2,1536]{2,0,1:T(8,128)(2,1)} collective-permute-done((bf16[96,2,1536]{2,0,1:T(8,128)(2,1)}, bf16[96,2,1536]{2,0,1:T(8,128)(2,1)}, u32[]{:S(2)}, u32[]{:S(2)}) %collective-permute-start.2) | collective-permute-done | bytes 589856 | tf_op jit(solution)/shard_map/ppermute | solution.py:78
  192.2 2.9 collective-permute-start.5
  197.1 9.1 %collective-permute-done.4 = bf16[96,2,1536]{2,0,1:T(8,128)(2,1)S(1)} collective-permute-done((bf16[96,2,1536]{2,0,1:T(8,128)(2,1)}, bf16[96,2,1536]{2,0,1:T(8,128)(2,1)S(1)}, u32[]{:S(2)}, u32[]{:S(2)}) %collective-permute-start.4) | collective-permute-done | bytes 589856 | tf_op jit(solution)/shard_map/ppermute | solution.py:78
  210.1 6.7 %collective-permute-done.6 = bf16[96,2,1536]{2,0,1:T(8,128)(2,1)S(1)} collective-permute-done((bf16[96,2,1536]{2,0,1:T(8,128)(2,1)S(1)}, bf16[96,2,1536]{2,0,1:T(8,128)(2,1)S(1)}, u32[]{:S(2)}, u32[]{:S(2)}) %collective-permute-start.6) | collective-permute-done | bytes 589856 | tf_op jit(solution)/shard_map/ppermute | solution.py:78
  217.6 5.0 %convolution_convert_fusion.4 = bf16[2,768,512]{2,1,0:T(8,128)(2,1)S(1)} fusion(bf16[768,2,1536]{2,0,1:T(8,128)(2,1)} %constant_dynamic-update-slice_fusion, bf16[2,512,1536]{2,1,0:T(8,128)(2,1)S(1)} %copy-done), kind=kOutput, calls=%fused_computation.21 | convolution fusion | flops 2416705536 | bytes 9437184 | tf_op jit(solution)/shard_map/rlf,lkf->lrk/dot_general | solution.py:105
  223.9 10.1 %all-to-all-start.2 = ((bf16[2,32,24,512]{3,2,0,1:T(8,128)(2,1)}), bf16[2,32,24,512]{3,2,0,1:T(8,128)(2,1)S(1)}, u32[]{:S(2)}, u32[]{:S(2)}) async-start(bf16[2,32,24,512]{3,2,0,1:T(8,128)(2,1)} %copy.68), calls=%async_computation.3 | async-start | bytes 3145728 | tf_op jit(solution)/shard_map/all_to_all | solution.py:114
  234.1 3.5 %convolution_convert_fusion.3 = bf16[2,768,512]{2,1,0:T(8,128)(2,1)S(1)} fusion(bf16[768,2,768]{2,0,1:T(8,128)(2,1)} %all-gather.2.cloned.1.call-done, bf16[2,768,512]{2,1,0:T(8,128)(2,1)} %param.10), kind=kOutput, calls=%fused_computation.20 | convolution fusion | flops 1208745984 | bytes 5505024 | tf_op jit(solution)/shard_map/rlf,lfk->lrk/dot_general | solution.py:86
  239.0 26.8 %all-to-all-done.2 = bf16[2,32,24,512]{3,2,0,1:T(8,128)(2,1)S(1)} async-done(((bf16[2,32,24,512]{3,2,0,1:T(8,128)(2,1)}), bf16[2,32,24,512]{3,2,0,1:T(8,128)(2,1)S(1)}, u32[]{:S(2)}, u32[]{:S(2)}) %all-to-all-start.2) | async-done | bytes 1572896 | tf_op jit(solution)/shard_map/all_to_all | solution.py:114
  265.8 5.6 %all-to-all-start.1 = ((bf16[2,32,24,512]{3,2,0,1:T(8,128)(2,1)}), bf16[2,32,24,512]{3,2,0,1:T(8,128)(2,1)S(1)}, u32[]{:S(2)}, u32[]{:S(2)}) async-start(bf16[2,32,24,512]{3,2,0,1:T(8,128)(2,1)} %copy.66), calls=%async_computation.2 | async-start | bytes 3145728 | tf_op jit(solution)/shard_map/all_to_all | solution.py:90
  272.1 7.3 %convolution_convert_fusion = bf16[2,512,1536]{2,1,0:T(8,128)(2,1)} fusion(bf16[2,768,512]{2,1,0:T(8,128)(2,1)} %bitcast.41, bf16[768,2,1536]{2,0,1:T(8,128)(2,1)} %constant_dynamic-update-slice_fusion), kind=kOutput, calls=%fused_computation.9 | convolution fusion | flops 2417491968 | bytes 9437184 | tf_op jit(solution)/shard_map/lrk,rlf->lkf/dot_general | solution.py:108
  279.4 2.6 convolution_convert_fusion.2
  283.1 19.9 %all-to-all-done.1 = bf16[2,32,24,512]{3,2,0,1:T(8,128)(2,1)S(1)} async-done(((bf16[2,32,24,512]{3,2,0,1:T(8,128)(2,1)}), bf16[2,32,24,512]{3,2,0,1:T(8,128)(2,1)S(1)}, u32[]{:S(2)}, u32[]{:S(2)}) %all-to-all-start.1) | async-done | bytes 1572896 | tf_op jit(solution)/shard_map/all_to_all | solution.py:90
  303.1 2.9 bitcast_reduce_fusion
  306.4 33.9 %psum.7 = f32[128,8]{1,0:T(8,128)S(1)} all-reduce(f32[128,8]{1,0:T(8,128)S(1)} %reshape.113), channel_id=1, replica_groups=mesh['dp'=8,'expert'=32] {'dp'}, use_global_device_ids=true, to_apply=%region_6.7 | all-reduce | flops 1024 | bytes 8192 | tf_op jit(solution)/shard_map/psum | solution.py:104
  (66 shorter events, 26.9 us)
Async XLA Ops:
  7.2 94.7 %copy-start = (bf16[2,512,1536]{2,1,0:T(8,128)(2,1)S(1)}, bf16[2,512,1536]{2,1,0:T(8,128)(2,1)}, u32[]{:S(2)}) copy-start(bf16[2,512,1536]{2,1,0:T(8,128)(2,1)} %param.9) | copy-start | bytes 9437188
  7.2 8.3 %copy-start.6 = (bf16[128,512]{1,0:T(8,128)(2,1)S(1)}, bf16[128,512]{1,0:T(8,128)(2,1)}, u32[]{:S(2)}) copy-start(bf16[128,512]{1,0:T(8,128)(2,1)} %param.11) | copy-start | bytes 393220
  7.2 154.0 %reduce-scatter.2.cloned.1.call-start = ((), (), s32[]{:S(2)}) async-start(), calls=%async_computation.4 | async-start | bytes 7962624 | tf_op jit(solution)/shard_map/reduce_scatter | solution.py:55
  101.7 4.4 %copy-start.2 = (bf16[1,2,32,24,512]{4,3,2,1,0:T(8,128)(2,1)}, bf16[1,2,32,24,512]{4,3,2,1,0:T(8,128)(2,1)S(1)}, u32[]{:S(2)}) copy-start(bf16[1,2,32,24,512]{4,3,2,1,0:T(8,128)(2,1)S(1)} %copy.63) | copy-start | bytes 4718596
  101.8 4.2 %copy-start.3 = (bf16[1,2,32,24,512]{4,3,2,1,0:T(8,128)(2,1)}, bf16[1,2,32,24,512]{4,3,2,1,0:T(8,128)(2,1)S(1)}, u32[]{:S(2)}) copy-start(bf16[1,2,32,24,512]{4,3,2,1,0:T(8,128)(2,1)S(1)} %copy.64) | copy-start | bytes 4718596
  101.8 4.2 %copy-start.8 = (bf16[2,768,512]{2,1,0:T(8,128)(2,1)S(1)}, bf16[2,768,512]{2,1,0:T(8,128)(2,1)}, u32[]{:S(2)}) copy-start(bf16[2,768,512]{2,1,0:T(8,128)(2,1)} %param.10) | copy-start | bytes 4718596
  115.3 118.7 %all-gather.2.cloned.1.call-start = ((), (), s32[]{:S(2)}) async-start(), calls=%async_computation.5 | async-start | bytes 2654208 | tf_op jit(solution)/shard_map/all_gather | solution.py:70
  166.9 10.6 %collective-permute-start = (bf16[96,2,1536]{2,0,1:T(8,128)(2,1)S(1)}, bf16[96,2,1536]{2,0,1:T(8,128)(2,1)}, u32[]{:S(2)}, u32[]{:S(2)}) collective-permute-start(bf16[96,2,1536]{2,0,1:T(8,128)(2,1)S(1)} %get-tuple-element.30), channel_id=1, source_target_pairs={{0,32},{32,64},{64,96},{96,128},{128,160},{160,192},{192,224},{224... | collective-permute-start | bytes 1769480 | tf_op jit(solution)/shard_map/ppermute | solution.py:78
  166.9 10.6 %collective-permute-start.1 = (bf16[96,2,1536]{2,0,1:T(8,128)(2,1)S(1)}, bf16[96,2,1536]{2,0,1:T(8,128)(2,1)}, u32[]{:S(2)}, u32[]{:S(2)}) collective-permute-start(bf16[96,2,1536]{2,0,1:T(8,128)(2,1)S(1)} %get-tuple-element.30), channel_id=1, source_target_pairs={{0,224},{32,0},{64,32},{96,64},{128,96},{160,128},{192,160},{224,1... | collective-permute-start | bytes 1769480 | tf_op jit(solution)/shard_map/ppermute | solution.py:81
  177.5 10.8 %collective-permute-start.2 = (bf16[96,2,1536]{2,0,1:T(8,128)(2,1)}, bf16[96,2,1536]{2,0,1:T(8,128)(2,1)}, u32[]{:S(2)}, u32[]{:S(2)}) collective-permute-start(bf16[96,2,1536]{2,0,1:T(8,128)(2,1)} %collective-permute-done), channel_id=1, source_target_pairs={{0,32},{32,64},{64,96},{96,128},{128,160},{160,192},{192,224},{224... | collective-permute-start | bytes 1769480 | tf_op jit(solution)/shard_map/ppermute | solution.py:78
  177.5 14.7 %collective-permute-start.3 = (bf16[96,2,1536]{2,0,1:T(8,128)(2,1)}, bf16[96,2,1536]{2,0,1:T(8,128)(2,1)}, u32[]{:S(2)}, u32[]{:S(2)}) collective-permute-start(bf16[96,2,1536]{2,0,1:T(8,128)(2,1)} %collective-permute-done.1), channel_id=1, source_target_pairs={{0,224},{32,0},{64,32},{96,64},{128,96},{160,128},{192,160},{224,1... | collective-permute-start | bytes 1769480 | tf_op jit(solution)/shard_map/ppermute | solution.py:81
  188.4 17.9 %collective-permute-start.4 = (bf16[96,2,1536]{2,0,1:T(8,128)(2,1)}, bf16[96,2,1536]{2,0,1:T(8,128)(2,1)S(1)}, u32[]{:S(2)}, u32[]{:S(2)}) collective-permute-start(bf16[96,2,1536]{2,0,1:T(8,128)(2,1)} %collective-permute-done.2), channel_id=1, source_target_pairs={{0,32},{32,64},{64,96},{96,128},{128,160},{160,192},{192,224},{224... | collective-permute-start | bytes 1769480 | tf_op jit(solution)/shard_map/ppermute | solution.py:78
  192.2 17.0 %collective-permute-start.5 = (bf16[96,2,1536]{2,0,1:T(8,128)(2,1)}, bf16[96,2,1536]{2,0,1:T(8,128)(2,1)S(1)}, u32[]{:S(2)}, u32[]{:S(2)}) collective-permute-start(bf16[96,2,1536]{2,0,1:T(8,128)(2,1)} %collective-permute-done.3), channel_id=1, source_target_pairs={{0,224},{32,0},{64,32},{96,64},{128,96},{160,128},{192,160},{224,1... | collective-permute-start | bytes 1769480 | tf_op jit(solution)/shard_map/ppermute | solution.py:81
  206.2 10.5 %collective-permute-start.6 = (bf16[96,2,1536]{2,0,1:T(8,128)(2,1)S(1)}, bf16[96,2,1536]{2,0,1:T(8,128)(2,1)S(1)}, u32[]{:S(2)}, u32[]{:S(2)}) collective-permute-start(bf16[96,2,1536]{2,0,1:T(8,128)(2,1)S(1)} %collective-permute-done.4), channel_id=1, source_target_pairs={{0,32},{32,64},{64,96},{96,128},{128,160},{160,192},{192,224},{224... | collective-permute-start | bytes 1769480 | tf_op jit(solution)/shard_map/ppermute | solution.py:78
  223.9 41.9 %all-to-all-start.2 = ((bf16[2,32,24,512]{3,2,0,1:T(8,128)(2,1)}), bf16[2,32,24,512]{3,2,0,1:T(8,128)(2,1)S(1)}, u32[]{:S(2)}, u32[]{:S(2)}) async-start(bf16[2,32,24,512]{3,2,0,1:T(8,128)(2,1)} %copy.68), calls=%async_computation.3 | async-start | bytes 3145728 | tf_op jit(solution)/shard_map/all_to_all | solution.py:114
  265.8 37.2 %all-to-all-start.1 = ((bf16[2,32,24,512]{3,2,0,1:T(8,128)(2,1)}), bf16[2,32,24,512]{3,2,0,1:T(8,128)(2,1)S(1)}, u32[]{:S(2)}, u32[]{:S(2)}) async-start(bf16[2,32,24,512]{3,2,0,1:T(8,128)(2,1)} %copy.66), calls=%async_computation.2 | async-start | bytes 3145728 | tf_op jit(solution)/shard_map/all_to_all | solution.py:90
  272.1 7.3 %copy-start.4 = (bf16[1,2,32,24,512]{4,3,2,1,0:T(8,128)(2,1)S(1)}, bf16[1,2,32,24,512]{4,3,2,1,0:T(8,128)(2,1)}, u32[]{:S(2)}) copy-start(bf16[1,2,32,24,512]{4,3,2,1,0:T(8,128)(2,1)} %copy-done.3) | copy-start | bytes 4718596
  272.1 7.3 %copy-start.7 = (bf16[768,2,768]{2,0,1:T(8,128)(2,1)S(1)}, bf16[768,2,768]{2,0,1:T(8,128)(2,1)}, u32[]{:S(2)}) copy-start(bf16[768,2,768]{2,0,1:T(8,128)(2,1)} %all-gather.2.cloned.1.call-done) | copy-start | bytes 7077892
  303.1 2.9 copy-start.5
  303.1 37.8 %copy-start.1 = (bf16[2,512,1536]{2,1,0:T(8,128)(2,1)S(1)}, bf16[2,512,1536]{2,1,0:T(8,128)(2,1)}, u32[]{:S(2)}) copy-start(bf16[2,512,1536]{2,1,0:T(8,128)(2,1)} %param.9) | copy-start | bytes 9437188
Sparse Core Ops, SparseCore 0:
  115.5 45.7 reduce-scatter.1
  180.6 29.4 all-gather.1
